TPU v7x, 512 devices: a whole 4x8x8 slice. The times are simulated.
512 devices in a mesh: pool: 64 (over x, z, core), mp: 8 (over y).
Axes of the slice: x: 4, y: 8, z: 8, core: 2. Of those that a mesh axis runs over, the one named last changes fastest.
Arguments:
- residual_in: bfloat16 [16384, 2048], P('pool', 'mp'), may hold values from -6 to 6
- mlp_branch: bfloat16 [16384, 2048], P('pool'), may hold values from -6 to 6
- norm_gain: float32 [2048], replicated, may hold values from 0.5 to 1.5
- norm_bias: float32 [2048], replicated, may hold values from -3 to 3
- w_qkv: bfloat16 [2048, 3, 2048], P('pool', None, 'mp'), may hold values from -0.125 to 0.125
- qkv_bias: float32 [3, 2048], P(None, 'mp'), may hold values from -3 to 3
- cache_pool: bfloat16 [3072, 2, 32, 2048], P('pool', None, None, 'mp'), as said below
- w_dense: bfloat16 [2048, 2048], P('mp', 'pool'), may hold values from -0.125 to 0.125
- dense_bias: float32 [2048], replicated, may hold values from -3 to 3
- next_gain: float32 [2048], replicated, may hold values from 0.5 to 1.5
- next_bias: float32 [2048], replicated, may hold values from -3 to 3
- w_next: bfloat16 [2048, 3, 2048], P('pool', None, 'mp'), may hold values from -0.125 to 0.125
- next_qkv_bias: float32 [3, 2048], P(None, 'mp'), may hold values from -3 to 3
- token_request: int32 [16384], P('pool'), may hold values from 0 to 255, as said below
- cache_len: int32 [256], P('pool'), may hold values from 0 to 1024, as said below
- block_table: int32 [256, 32], P('pool'), may hold values from 0 to 3071, as said below
Outputs:
- hidden_out: bfloat16 [16384, 2048], P('pool', 'mp')
- next_qkv: bfloat16 [16384, 3, 2048], P('pool', None, 'mp')
Inputs may be any that keep to these rules, and one draw needn't show every extreme that they name: `token_request`: the 256 tokens of index i of pool belong to the requests i * 4 to (i+1) * 4 - 1, each request's tokens in one run, in increasing order, each request with at least one token. `cache_len`: 0 for a fresh prompt; some request has exactly 1024. `block_table`: block b is held by index b // 48 of pool; a block may appear in several lists; entries at or past a request's cached blocks are padding. Of the 128 entries of the requests of one index of pool, exactly 2 name blocks held by each index of pool. `cache_pool`: cached keys and values.
All inputs are finite; a program needn't handle non-finite values.
Results may differ from a plain program's by a relative error of at most 0.015.
Values may be sent and summed in bfloat16 or wider, within the bound.
No kernel may reach another device: no remote copies, remote signals or barrier semaphores. Data moves between devices by JAX's collectives and lax.ppermute only.
A program may use at most 128 MiB of HBM per device.

v0:
```python
import jax
import jax.numpy as jnp
from jax import lax
from jax.sharding import PartitionSpec as P

HEAD_DIM = 64
ROT = 32
epsilon = 1e-05


def layer_norm(row_data, gain_vec, bias_vec):
    values = row_data.astype(jnp.float32)
    row_mean = jnp.mean(values, axis=-1, keepdims=True)
    centered = values - row_mean
    spread = jnp.mean(centered * centered, axis=-1, keepdims=True)
    return centered * lax.rsqrt(spread + epsilon) * gain_vec + bias_vec


def rotate(head_rows, positions):
    half_rot = ROT // 2
    inverse = 10000.0 ** (-2.0 * jnp.arange(half_rot, dtype=jnp.float32) / ROT)
    angles = positions.astype(jnp.float32)[:, None] * inverse[None, :]
    cosine = jnp.cos(angles)[:, None, :]
    sine = jnp.sin(angles)[:, None, :]
    lower = head_rows[..., :half_rot]
    upper = head_rows[..., half_rot:ROT]
    return jnp.concatenate(
        [lower * cosine - upper * sine, upper * cosine + lower * sine, head_rows[..., ROT:]],
        axis=-1,
    )


def run_starts(token_request):
    tok_total = token_request.shape[0]
    token_index = jnp.arange(tok_total, dtype=jnp.int32)
    change = jnp.concatenate([jnp.ones((1,), dtype=bool), token_request[1:] != token_request[:-1]])
    return (token_index, lax.cummax(jnp.where(change, token_index, 0), axis=0))


def row_folder(left_rows, running, w_piece):
    columns_part = lax.slice_in_dim(left_rows, 0, w_piece.shape[0], axis=1)
    return running + jnp.dot(
        columns_part, w_piece.reshape(w_piece.shape[0], -1), preferred_element_type=jnp.float32
    )


def local(
    residual_in,
    mlp_branch,
    norm_gain,
    norm_bias,
    w_qkv,
    qkv_bias,
    cache_pool,
    w_dense,
    dense_bias,
    next_gain,
    next_bias,
    w_next,
    next_qkv_bias,
    token_request,
    cache_len,
    block_table,
):
    full_rows = lax.all_gather(residual_in, "mp", axis=1, tiled=True)
    tok_count = full_rows.shape[0]
    col_width = w_qkv.shape[2]
    head_count = col_width // HEAD_DIM
    normed = layer_norm(full_rows, norm_gain, norm_bias).astype(jnp.bfloat16)
    empty_sum = jnp.zeros((tok_count, 3 * col_width), jnp.float32)
    projected = row_folder(normed, empty_sum, lax.all_gather(w_qkv, "pool", axis=0, tiled=True))
    projected = (projected + qkv_bias.reshape(1, 3 * col_width)).reshape(tok_count, 3, col_width)
    token_index, starts = run_starts(token_request)
    request_count = cache_len.shape[0]
    local_req = token_request - request_count * lax.axis_index("pool")
    request_ids = jnp.arange(request_count, dtype=jnp.int32)
    request_match = local_req[:, None] == request_ids[None, :]
    cached_here = jnp.sum(jnp.where(request_match, cache_len[None, :], 0), axis=1)
    positions = cached_here + token_index - starts
    query = rotate(projected[:, 0].reshape(tok_count, head_count, HEAD_DIM), positions).astype(
        jnp.bfloat16
    )
    key_new = rotate(projected[:, 1].reshape(tok_count, head_count, HEAD_DIM), positions).astype(
        jnp.bfloat16
    )
    value_new = projected[:, 2].reshape(tok_count, head_count, HEAD_DIM).astype(jnp.bfloat16)
    pool_count = lax.axis_size("pool")
    blocks_here = cache_pool.shape[0]
    entries = block_table.reshape(-1)
    holder_order = jnp.argsort(entries // blocks_here, stable=True)
    slot_ids = (entries % blocks_here)[holder_order].reshape(pool_count, -1)
    wanted = lax.all_to_all(slot_ids, "pool", split_axis=0, concat_axis=0, tiled=True)
    packed = cache_pool[wanted.reshape(-1)].reshape((pool_count, -1) + cache_pool.shape[1:])
    arrived = lax.all_to_all(packed, "pool", split_axis=0, concat_axis=0, tiled=True)
    table_blocks = arrived.reshape((-1,) + cache_pool.shape[1:])[jnp.argsort(holder_order)]
    span = block_table.shape[1] * cache_pool.shape[2]
    slot_total = request_count * span
    cached_keys = table_blocks[:, 0].reshape(slot_total, head_count, HEAD_DIM)
    cached_values = table_blocks[:, 1].reshape(slot_total, head_count, HEAD_DIM)
    slot_index = jnp.arange(slot_total, dtype=jnp.int32)
    slot_req = slot_index // span
    slot_len = jnp.repeat(cache_len, span, total_repeat_length=slot_total)
    cache_ok = (slot_req[None, :] == local_req[:, None]) & (slot_index % span < slot_len)[None, :]
    new_ok = (token_request[None, :] == token_request[:, None]) & (
        token_index[None, :] <= token_index[:, None]
    )
    allowed = jnp.concatenate([cache_ok, new_ok], axis=1)
    key_all = jnp.concatenate([cached_keys, key_new], axis=0).transpose(1, 0, 2)
    value_all = jnp.concatenate([cached_values, value_new], axis=0).transpose(1, 0, 2)
    score_scale = HEAD_DIM ** (-0.5)

    def one_head(operands):
        q_head, k_head, v_head = operands
        scores = (
            jnp.einsum("qd,kd->qk", q_head, k_head, preferred_element_type=jnp.float32)
            * score_scale
        )
        scores = jnp.where(allowed, scores, -1e30)
        row_max = jnp.max(scores, axis=1, keepdims=True)
        weights = jnp.exp(scores - row_max)
        probs = (weights / jnp.sum(weights, axis=1, keepdims=True)).astype(jnp.bfloat16)
        return jnp.dot(probs, v_head, preferred_element_type=jnp.float32).astype(jnp.bfloat16)

    mixed = lax.map(one_head, (query.transpose(1, 0, 2), key_all, value_all))
    attended = mixed.transpose(1, 0, 2).reshape(tok_count, col_width)
    partial_out = jnp.dot(
        attended,
        lax.all_gather(w_dense, "pool", axis=1, tiled=True),
        preferred_element_type=jnp.float32,
    )
    mp_index = lax.axis_index("mp")
    dense_total = lax.psum(partial_out.astype(jnp.bfloat16), "mp").astype(jnp.float32)
    whole_hidden = (
        full_rows.astype(jnp.float32) + dense_total + dense_bias + mlp_branch.astype(jnp.float32)
    ).astype(jnp.bfloat16)
    hidden_out = lax.dynamic_slice_in_dim(whole_hidden, mp_index * col_width, col_width, 1)
    normed_next = layer_norm(whole_hidden, next_gain, next_bias).astype(jnp.bfloat16)
    next_raw = row_folder(
        normed_next, empty_sum, lax.all_gather(w_next, "pool", axis=0, tiled=True)
    )
    next_qkv = (
        (next_raw + next_qkv_bias.reshape(1, 3 * col_width))
        .astype(jnp.bfloat16)
        .reshape(tok_count, 3, col_width)
    )
    return (hidden_out, next_qkv)


def solution(mesh):
    in_specs = (
        P("pool", "mp"),
        P("pool", None),
        P(),
        P(),
        P("pool", None, "mp"),
        P(None, "mp"),
        P("pool", None, None, "mp"),
        P("mp", "pool"),
        P(),
        P(),
        P(),
        P("pool", None, "mp"),
        P(None, "mp"),
        P("pool"),
        P("pool"),
        P("pool", None),
    )
    out_specs = (P("pool", "mp"), P("pool", None, "mp"))
    return jax.shard_map(local, mesh=mesh, in_specs=in_specs, out_specs=out_specs, check_vma=False)
```

profile of v0, /device:TPU:2, one launch (start us, length us, event | category | flops | bytes accessed | tf_op | source)
XLA Modules:
  0.0 420.4 jit_solution(15002149205869213757)
XLA Ops:
  10.3 2.5 sort.34
  14.2 22.3 %all_to_all.14 = s32[64,1,2]{2,1,0:T(1,128)S(1)} all-to-all(s32[64,1,2]{2,1,0:T(1,128)S(1)} %bitcast.83), channel_id=1, replica_groups=mesh['pool'=64,'mp'=8] {'pool'}, dimensions={0} | all-to-all | bytes 1024 | tf_op jit(solution)/shard_map/all_to_all | solution.py:92
  37.9 2.8 gather_fusion.1
  40.7 6.6 %all-to-all-start.1 = ((bf16[64,2,2,32,256]{4,3,2,1,0:T(8,128)(2,1)}), bf16[64,2,2,32,256]{4,3,2,1,0:T(8,128)(2,1)}, u32[]{:S(2)}, u32[]{:S(2)}) async-start(bf16[64,2,2,32,256]{4,3,2,1,0:T(8,128)(2,1)} %bitcast.71), calls=%async_computation.1 | async-start | bytes 8388608 | tf_op jit(solution)/shard_map/all_to_all | solution.py:94
  49.6 2.5 sort.35
  53.1 2.5 fusion.51
  58.2 1.6 fusion.22
  59.9 97.4 %all-gather.7.cloned.1.call-done = bf16[2048,3,256]{2,0,1:T(8,128)(2,1)} async-done(((bf16[32,3,256]{2,0,1:T(8,128)(2,1)}), bf16[2048,3,256]{2,0,1:T(8,128)(2,1)}) %all-gather.7.cloned.1.call-update) | async-done | bytes 3145744 | tf_op jit(solution)/shard_map/all_gather | solution.py:71
  157.3 4.7 %copy.69 = bf16[2048,3,256]{0,2,1:T(8,128)(2,1)} copy(bf16[2048,3,256]{2,0,1:T(8,128)(2,1)} %all-gather.7.cloned.1.call-done) | data formatting | bytes 6291456 | tf_op jit(solution)/shard_map/all_gather | solution.py:71
  162.1 4.0 convolution_add_fusion.1
  168.0 5.0 %gather_fusion.2 = bf16[128,2,32,256]{3,2,1,0:T(8,128)(2,1)} fusion(bf16[128,2,32,256]{3,2,1,0:T(8,128)(2,1)} %bitcast.13, s32[1024]{0:T(1024)S(1)} %pad_clamp_fusion), kind=kCustom, calls=%fused_computation.2 | custom fusion | bytes 8389120 | tf_op jit(solution)/shard_map/gather | solution.py:95
  173.0 4.7 %fusion.58 = (bf16[128,1,32,256]{3,2,1,0:T(8,128)(2,1)}, bf16[128,1,32,256]{3,2,1,0:T(8,128)(2,1)}) fusion(bf16[128,2,32,256]{3,2,1,0:T(8,128)(2,1)} %gather_fusion.2), kind=kLoop, calls=%fused_computation.109 | loop fusion | bytes 8388608 | tf_op jit(solution)/shard_map/slice | solution.py:99
  177.6 7.1 %reshape_squeeze.14 = bf16[4096,4,64]{2,1,0:T(4,128)(2,1)} reshape(bf16[128,1,32,256]{3,2,1,0:T(8,128)(2,1)} %get-tuple-element.110) | data formatting | bytes 4194304 | tf_op jit(solution)/shard_map/reshape;squeeze | solution.py:98
  184.7 17.6 %maximum_bitcast_fusion = bf16[4,4352,64]{2,0,1:T(4,128)(2,1)S(1)} fusion(bf16[256,4,64]{2,1,0:T(4,128)(2,1)S(1)} %copy.72, bf16[4096,4,64]{2,1,0:T(4,128)(2,1)} %reshape_squeeze.14), kind=kLoop, calls=%fused_computation.20 | loop fusion | flops 1114112 | bytes 4456448 | tf_op jit(solution)/shard_map/transpose | solution.py:108
  202.4 2.7 copy.75
  205.1 7.1 %reshape_squeeze.16 = bf16[4096,4,64]{2,1,0:T(4,128)(2,1)} reshape(bf16[128,1,32,256]{3,2,1,0:T(8,128)(2,1)} %get-tuple-element.109) | data formatting | bytes 4194304 | tf_op jit(solution)/shard_map/reshape;squeeze | solution.py:99
  212.1 17.6 %maximum_bitcast_fusion.1 = bf16[4,4352,64]{2,0,1:T(4,128)(2,1)S(1)} fusion(bf16[256,4,64]{2,1,0:T(4,128)(2,1)S(1)} %copy.73, bf16[4096,4,64]{2,1,0:T(4,128)(2,1)} %reshape_squeeze.16), kind=kLoop, calls=%fused_computation.21 | loop fusion | flops 1114112 | bytes 4456448 | tf_op jit(solution)/shard_map/transpose | solution.py:109
  229.8 2.7 copy.76
  232.5 21.9 %while.11 = (s32[]{:T(128)}, bf16[4,256,64]{1,2,0:T(8,128)(2,1)S(1)}, bf16[4,256,64]{1,2,0:T(8,128)(2,1)S(1)}, bf16[4,4352,64]{2,1,0:T(8,128)(2,1)}, pred[256,43...) while((s32[]{:T(128)}, bf16[4,256,64]{1,2,0:T(8,128)(2,1)S(1)}, ...), condition=%wide.region_10.11_spmd, body=%wide.region_7.10_spmd.sunk | while | flops 294141440 | bytes 16784460 | solution.py:124
  232.5 2.4 fusion.70
  235.6 2.4 fusion.72
  238.0 2.3 fusion.70
  241.1 2.4 fusion.72
  243.4 2.3 fusion.70
  246.5 2.4 fusion.72
  248.9 2.3 fusion.70
  252.0 2.4 fusion.72
  254.4 2.7 convolution_convert_fusion
  257.2 68.4 %all-gather.11.cloned.1.call-done = bf16[2048,3,256]{2,0,1:T(8,128)(2,1)} async-done(((bf16[32,3,256]{2,0,1:T(8,128)(2,1)}), bf16[2048,3,256]{2,0,1:T(8,128)(2,1)}) %all-gather.11.cloned.1.call-update) | async-done | bytes 3145744 | tf_op jit(solution)/shard_map/all_gather | solution.py:139
  325.6 4.7 %copy.77 = bf16[2048,3,256]{0,2,1:T(8,128)(2,1)} copy(bf16[2048,3,256]{2,0,1:T(8,128)(2,1)} %all-gather.11.cloned.1.call-done) | data formatting | bytes 6291456 | tf_op jit(solution)/shard_map/all_gather | solution.py:139
  330.3 76.7 %all-reduce.2.cloned.1.call-done = bf16[256,2048]{1,0:T(8,128)(2,1)} async-done(((bf16[256,2048]{1,0:T(8,128)(2,1)}), bf16[256,2048]{1,0:T(8,128)(2,1)}) %all-reduce.2.cloned.1.call-update) | async-done | bytes 1048592 | tf_op jit(solution)/shard_map/psum | solution.py:132
  407.0 2.0 convert_reduce_fusion.1
  (112 shorter events, 21.3 us)
Async XLA Ops:
  7.2 30.8 %copy-start = (bf16[48,2,32,256]{3,2,1,0:T(8,128)(2,1)S(1)}, bf16[48,2,32,256]{3,2,1,0:T(8,128)(2,1)}, u32[]{:S(2)}) copy-start(bf16[48,2,32,256]{3,2,1,0:T(8,128)(2,1)} %param.26) | copy-start | bytes 4718596
  7.2 49.6 %all-gather.5.cloned.1.call-start = ((), (), s32[]{:S(2)}) async-start(), calls=%async_computation.2 | async-start | bytes 1179648 | tf_op jit(solution)/shard_map/all_gather | solution.py:65
  7.9 149.4 %all-gather.7.cloned.1.call-start = ((), (), s32[]{:S(2)}) async-start(), calls=%async_computation.3 | async-start | bytes 3194880 | tf_op jit(solution)/shard_map/all_gather | solution.py:71
  40.7 8.2 %copy-start.10 = (f32[3,256]{1,0:T(4,128)S(1)}, f32[3,256]{1,0:T(4,128)}, u32[]{:S(2)}) copy-start(f32[3,256]{1,0:T(4,128)} %param.25) | copy-start | bytes 9220
  40.7 8.3 %copy-start.7 = (s32[256]{0:T(256)S(1)}, s32[256]{0:T(256)}, u32[]{:S(2)}) copy-start(s32[256]{0:T(256)} %param.33) | copy-start | bytes 3076
  40.7 11.5 %copy-start.8 = (s32[4]{0:T(128)S(1)}, s32[4]{0:T(128)}, u32[]{:S(2)}) copy-start(s32[4]{0:T(128)} %param.34) | copy-start | bytes 52
  40.7 12.3 %copy-start.12 = (pred[4096]{0:T(1024)(128)(4,1)S(1)}, pred[4096]{0:T(1024)(128)(4,1)}, u32[]{:S(2)}) copy-start(pred[4096]{0:T(1024)(128)(4,1)} %constant.223) | copy-start | bytes 12292
  40.7 12.3 %copy-start.13 = (pred[4096]{0:T(1024)(128)(4,1)S(1)}, pred[4096]{0:T(1024)(128)(4,1)}, u32[]{:S(2)}) copy-start(pred[4096]{0:T(1024)(128)(4,1)} %constant.224) | copy-start | bytes 12292
  40.7 12.3 %copy-start.14 = (pred[4096]{0:T(1024)(128)(4,1)S(1)}, pred[4096]{0:T(1024)(128)(4,1)}, u32[]{:S(2)}) copy-start(pred[4096]{0:T(1024)(128)(4,1)} %constant.225) | copy-start | bytes 12292
  40.7 127.2 %all-to-all-start.1 = ((bf16[64,2,2,32,256]{4,3,2,1,0:T(8,128)(2,1)}), bf16[64,2,2,32,256]{4,3,2,1,0:T(8,128)(2,1)}, u32[]{:S(2)}, u32[]{:S(2)}) async-start(bf16[64,2,2,32,256]{4,3,2,1,0:T(8,128)(2,1)} %bitcast.71), calls=%async_computation.1 | async-start | bytes 8388608 | tf_op jit(solution)/shard_map/all_to_all | solution.py:94
  47.4 207.0 %all-gather.9.cloned.1.call-start = ((), (), s32[]{:S(2)}) async-start(), calls=%async_computation.4 | async-start | bytes 1064960 | tf_op jit(solution)/shard_map/all_gather | solution.py:128
  48.1 277.5 %all-gather.11.cloned.1.call-start = ((), (), s32[]{:S(2)}) async-start(), calls=%async_computation.6 | async-start | bytes 3194880 | tf_op jit(solution)/shard_map/all_gather | solution.py:139
  48.7 358.3 %all-reduce.2.cloned.1.call-start = ((), (), s32[]{:S(2)}) async-start(), calls=%async_computation.5 | async-start | bytes 2097152 | tf_op jit(solution)/shard_map/psum | solution.py:132
  59.9 102.2 %copy-start.2 = (bf16[256,2048]{1,0:T(8,128)(2,1)S(1)}, bf16[256,2048]{1,0:T(8,128)(2,1)}, u32[]{:S(2)}) copy-start(bf16[256,2048]{1,0:T(8,128)(2,1)} %all-gather.5.cloned.1.call-done) | copy-start | bytes 3145732
  59.9 102.2 %copy-start.15 = (f32[2048]{0:T(1024)S(1)}, f32[2048]{0:T(1024)}, u32[]{:S(2)}) copy-start(f32[2048]{0:T(1024)} %param.23) | copy-start | bytes 24580
  59.9 102.2 %copy-start.16 = (f32[2048]{0:T(1024)S(1)}, f32[2048]{0:T(1024)}, u32[]{:S(2)}) copy-start(f32[2048]{0:T(1024)} %param.22) | copy-start | bytes 24580
  229.8 2.7 copy-start.6
  254.4 2.8 copy-start.11
  257.2 149.8 %copy-start.5 = (bf16[256,2048]{1,0:T(8,128)(2,1)S(1)}, bf16[256,2048]{1,0:T(8,128)(2,1)}, u32[]{:S(2)}) copy-start(bf16[256,2048]{1,0:T(8,128)(2,1)} %param.21) | copy-start | bytes 3145732
  257.2 149.8 %copy-start.9 = (f32[2048]{0:T(1024)S(1)}, f32[2048]{0:T(1024)}, u32[]{:S(2)}) copy-start(f32[2048]{0:T(1024)} %param.28) | copy-start | bytes 24580
  330.3 79.8 %copy-start.17 = (f32[2048]{0:T(1024)S(1)}, f32[2048]{0:T(1024)}, u32[]{:S(2)}) copy-start(f32[2048]{0:T(1024)} %param.30) | copy-start | bytes 24580
  330.3 79.8 %copy-start.18 = (f32[2048]{0:T(1024)S(1)}, f32[2048]{0:T(1024)}, u32[]{:S(2)}) copy-start(f32[2048]{0:T(1024)} %param.29) | copy-start | bytes 24580
  407.0 3.0 copy-start.4
  409.1 1.0 copy-start.3
  409.5 4.4 %copy-start.1 = (bf16[48,2,32,256]{3,2,1,0:T(8,128)(2,1)S(1)}, bf16[48,2,32,256]{3,2,1,0:T(8,128)(2,1)}, u32[]{:S(2)}) copy-start(bf16[48,2,32,256]{3,2,1,0:T(8,128)(2,1)} %param.26) | copy-start | bytes 4718596
Sparse Core Ops, SparseCore 0:
  10.0 46.6 all-gather.4
  60.1 97.1 all-gather.6
  160.7 80.2 all-gather.8
  244.2 81.3 all-gather.10
  327.8 79.2 all-reduce.1
where the time goes:
time: 422 us; the launch traced here: 420 us
  waiting for transfers between devices  245 us (58%)
  other arithmetic  55.4 us (13%)
  local copies, waits for them, and re-layouts  49.6 us (12%)
  matrix products  26.7 us (6%)
  blocking collectives  22.3 us (5%)
  between operations  14.2 us (3%)
  starting transfers between devices  7.01 us (2%)
    all_gather x1, waiting for transfers between devices, local(): lax.all_gather(w_qkv, 'pool', axis=0, tiled=True)  97.4 us
    psum x1, waiting for transfers between devices, local(): lax.psum(partial_out.astype(jnp.bfloat16), 'mp').astype(jnp.float32)  76.7 us
    all_gather x1, waiting for transfers between devices, local(): lax.all_gather(w_next, 'pool', axis=0, tiled=True)  68.4 us
    all_to_all x1, blocking collectives, local(): lax.all_to_all(slot_ids, 'pool', split_axis=0, concat_axis=0, tiled=True)  22.3 us
    transpose x1, other arithmetic, local(): jnp.concatenate([cached_values, value_new], axis=0).transpose(1, 0, 2)  17.6 us
    transpose x1, other arithmetic, local(): key_all = jnp.concatenate([cached_keys, key_new], axis=0).transpose(1, 0, 2)  17.6 us
    dot_general x4, matrix products, one_head(): jnp.dot(probs, v_head, preferred_element_type=jnp.float32)  9.42 us
    dot_general x4, matrix products, one_head(): jnp.einsum('qd,kd->qk', q_head, k_head, preferred_element_type=jnp.float32)  9.39 us
  transfers between devices with their start and end apart: 6, of which 4 were waited for; matrix products, arithmetic and copies ran while one was open for 30% of the time, Pallas kernels for 0%

commit v1 on v0

--- a/solution.py
+++ b/solution.py
@@ -129,7 +129,9 @@
         preferred_element_type=jnp.float32,
     )
     mp_index = lax.axis_index("mp")
-    dense_total = lax.psum(partial_out.astype(jnp.bfloat16), "mp").astype(jnp.float32)
+    dense_total = jnp.sum(lax.all_gather(partial_out.astype(jnp.bfloat16), "mp"), axis=0).astype(
+        jnp.float32
+    )
     whole_hidden = (
         full_rows.astype(jnp.float32) + dense_total + dense_bias + mlp_branch.astype(jnp.float32)
     ).astype(jnp.bfloat16)

time: 422 us -> 443 us (1.050)
  the two profiles are of different devices: /device:TPU:2 before, /device:TPU:1 now
where the time goes in v1:
time: 443 us; the launch traced here: 442 us
  waiting for transfers between devices  260 us (59%)
  other arithmetic  60.6 us (14%)
  local copies, waits for them, and re-layouts  49.5 us (11%)
  matrix products  26.7 us (6%)
  blocking collectives  23.9 us (5%)
  between operations  14.2 us (3%)
  starting transfers between devices  6.2 us (1%)
    all_gather x1, waiting for transfers between devices, local(): lax.all_gather(w_qkv, 'pool', axis=0, tiled=True)  98.1 us
    all_gather x1, waiting for transfers between devices, local(): lax.all_gather(partial_out.astype(jnp.bfloat16), 'mp')  90.1 us
    all_gather x1, waiting for transfers between devices, local(): lax.all_gather(w_next, 'pool', axis=0, tiled=True)  69.4 us
    all_to_all x1, blocking collectives, local(): lax.all_to_all(slot_ids, 'pool', split_axis=0, concat_axis=0, tiled=True)  23.9 us
    transpose x1, other arithmetic, local(): key_all = jnp.concatenate([cached_keys, key_new], axis=0).transpose(1, 0, 2)  17.6 us
    transpose x1, other arithmetic, local(): jnp.concatenate([cached_values, value_new], axis=0).transpose(1, 0, 2)  17.6 us
    dot_general x4, matrix products, one_head(): jnp.dot(probs, v_head, preferred_element_type=jnp.float32)  9.41 us
    dot_general x4, matrix products, one_head(): jnp.einsum('qd,kd->qk', q_head, k_head, preferred_element_type=jnp.float32)  9.38 us
  transfers between devices with their start and end apart: 6, of which 3 were waited for; matrix products, arithmetic and copies ran while one was open for 28% of the time, Pallas kernels for 0%

profile of v1, /device:TPU:1, one launch (start us, length us, event | category | flops | bytes accessed | tf_op | source)
XLA Modules:
  0.0 441.5 jit_solution(10922649553515001867)
XLA Ops:
  10.3 2.5 sort.34
  14.2 23.9 %all_to_all.14 = s32[64,1,2]{2,1,0:T(1,128)S(1)} all-to-all(s32[64,1,2]{2,1,0:T(1,128)S(1)} %bitcast.85), channel_id=1, replica_groups=mesh['pool'=64,'mp'=8] {'pool'}, dimensions={0} | all-to-all | bytes 1024 | tf_op jit(solution)/shard_map/all_to_all | solution.py:92
  39.6 2.8 gather_fusion.1
  42.4 5.8 %all-to-all-start.1 = ((bf16[64,2,2,32,256]{4,3,2,1,0:T(8,128)(2,1)}), bf16[64,2,2,32,256]{4,3,2,1,0:T(8,128)(2,1)}, u32[]{:S(2)}, u32[]{:S(2)}) async-start(bf16[64,2,2,32,256]{4,3,2,1,0:T(8,128)(2,1)} %bitcast.72), calls=%async_computation.1 | async-start | bytes 8388608 | tf_op jit(solution)/shard_map/all_to_all | solution.py:94
  50.4 2.5 sort.35
  53.9 2.5 fusion.51
  60.7 98.1 %all-gather.9.cloned.1.call-done = bf16[2048,3,256]{2,0,1:T(8,128)(2,1)} async-done(((bf16[32,3,256]{2,0,1:T(8,128)(2,1)}), bf16[2048,3,256]{2,0,1:T(8,128)(2,1)}) %all-gather.9.cloned.1.call-update) | async-done | bytes 3145744 | tf_op jit(solution)/shard_map/all_gather | solution.py:71
  158.8 4.7 %copy.69 = bf16[2048,3,256]{0,2,1:T(8,128)(2,1)} copy(bf16[2048,3,256]{2,0,1:T(8,128)(2,1)} %all-gather.9.cloned.1.call-done) | data formatting | bytes 6291456 | tf_op jit(solution)/shard_map/all_gather | solution.py:71
  163.5 4.0 convolution_add_fusion.1
  169.5 5.0 %gather_fusion.2 = bf16[128,2,32,256]{3,2,1,0:T(8,128)(2,1)} fusion(bf16[128,2,32,256]{3,2,1,0:T(8,128)(2,1)} %bitcast.13, s32[1024]{0:T(1024)S(1)} %pad_clamp_fusion), kind=kCustom, calls=%fused_computation.2 | custom fusion | bytes 8389120 | tf_op jit(solution)/shard_map/gather | solution.py:95
  174.4 4.7 %fusion.58 = (bf16[128,1,32,256]{3,2,1,0:T(8,128)(2,1)}, bf16[128,1,32,256]{3,2,1,0:T(8,128)(2,1)}) fusion(bf16[128,2,32,256]{3,2,1,0:T(8,128)(2,1)} %gather_fusion.2), kind=kLoop, calls=%fused_computation.109 | loop fusion | bytes 8388608 | tf_op jit(solution)/shard_map/slice | solution.py:99
  179.1 7.1 %reshape_squeeze.14 = bf16[4096,4,64]{2,1,0:T(4,128)(2,1)} reshape(bf16[128,1,32,256]{3,2,1,0:T(8,128)(2,1)} %get-tuple-element.110) | data formatting | bytes 4194304 | tf_op jit(solution)/shard_map/reshape;squeeze | solution.py:98
  186.2 17.6 %maximum_bitcast_fusion = bf16[4,4352,64]{2,0,1:T(4,128)(2,1)S(1)} fusion(bf16[256,4,64]{2,1,0:T(4,128)(2,1)S(1)} %copy.72, bf16[4096,4,64]{2,1,0:T(4,128)(2,1)} %reshape_squeeze.14), kind=kLoop, calls=%fused_computation.20 | loop fusion | flops 1114112 | bytes 4456448 | tf_op jit(solution)/shard_map/transpose | solution.py:108
  203.9 2.7 copy.75
  206.5 7.1 %reshape_squeeze.16 = bf16[4096,4,64]{2,1,0:T(4,128)(2,1)} reshape(bf16[128,1,32,256]{3,2,1,0:T(8,128)(2,1)} %get-tuple-element.109) | data formatting | bytes 4194304 | tf_op jit(solution)/shard_map/reshape;squeeze | solution.py:99
  213.6 17.6 %maximum_bitcast_fusion.1 = bf16[4,4352,64]{2,0,1:T(4,128)(2,1)S(1)} fusion(bf16[256,4,64]{2,1,0:T(4,128)(2,1)S(1)} %copy.73, bf16[4096,4,64]{2,1,0:T(4,128)(2,1)} %reshape_squeeze.16), kind=kLoop, calls=%fused_computation.21 | loop fusion | flops 1114112 | bytes 4456448 | tf_op jit(solution)/shard_map/transpose | solution.py:109
  231.3 2.7 copy.76
  234.0 21.9 %while.11 = (s32[]{:T(128)}, bf16[4,256,64]{1,2,0:T(8,128)(2,1)S(1)}, bf16[4,256,64]{1,2,0:T(8,128)(2,1)S(1)}, bf16[4,4352,64]{2,1,0:T(8,128)(2,1)}, pred[256,43...) while((s32[]{:T(128)}, bf16[4,256,64]{1,2,0:T(8,128)(2,1)S(1)}, ...), condition=%wide.region_10.11_spmd, body=%wide.region_7.10_spmd.sunk | while | flops 294141440 | bytes 16784460 | solution.py:124
  234.0 2.3 fusion.70
  237.1 2.4 fusion.72
  239.4 2.3 fusion.70
  242.5 2.3 fusion.72
  244.9 2.3 fusion.70
  248.0 2.4 fusion.72
  250.4 2.3 fusion.70
  253.5 2.4 fusion.72
  255.9 2.7 convolution_convert_fusion
  258.7 69.4 %all-gather.13.cloned.1.call-done = bf16[2048,3,256]{2,0,1:T(8,128)(2,1)} async-done(((bf16[32,3,256]{2,0,1:T(8,128)(2,1)}), bf16[2048,3,256]{2,0,1:T(8,128)(2,1)}) %all-gather.13.cloned.1.call-update) | async-done | bytes 3145744 | tf_op jit(solution)/shard_map/all_gather | solution.py:141
  328.0 4.7 %copy.77 = bf16[2048,3,256]{0,2,1:T(8,128)(2,1)} copy(bf16[2048,3,256]{2,0,1:T(8,128)(2,1)} %all-gather.13.cloned.1.call-done) | data formatting | bytes 6291456 | tf_op jit(solution)/shard_map/all_gather | solution.py:141
  332.7 90.1 %all-gather.15.cloned.1.call-done = bf16[2048,2048]{1,0:T(8,128)(2,1)} async-done(((bf16[256,2048]{1,0:T(8,128)(2,1)}), bf16[2048,2048]{1,0:T(8,128)(2,1)}) %all-gather.15.cloned.1.call-update) | async-done | bytes 8388624 | tf_op jit(solution)/shard_map/all_gather | solution.py:132
  422.8 5.2 %reduce_sum.69 = bf16[256,2048]{1,0:T(8,128)(2,1)S(1)} reduce(bf16[8,256,2048]{2,1,0:T(8,128)(2,1)} %bitcast.73, bf16[]{:T(256)} %constant.191.clone.1), dimensions={0}, to_apply=%region_11.12 | reduce | flops 3670016 | bytes 9437186 | tf_op jit(solution)/shard_map/reduce_sum | solution.py:132
  428.1 2.0 convert_reduce_fusion.1
  (111 shorter events, 22.9 us)
Async XLA Ops:
  7.2 32.4 %copy-start = (bf16[48,2,32,256]{3,2,1,0:T(8,128)(2,1)S(1)}, bf16[48,2,32,256]{3,2,1,0:T(8,128)(2,1)}, u32[]{:S(2)}) copy-start(bf16[48,2,32,256]{3,2,1,0:T(8,128)(2,1)} %param.26) | copy-start | bytes 4718596
  7.2 50.4 %all-gather.7.cloned.1.call-start = ((), (), s32[]{:S(2)}) async-start(), calls=%async_computation.2 | async-start | bytes 1179648 | tf_op jit(solution)/shard_map/all_gather | solution.py:65
  7.9 150.9 %all-gather.9.cloned.1.call-start = ((), (), s32[]{:S(2)}) async-start(), calls=%async_computation.3 | async-start | bytes 3194880 | tf_op jit(solution)/shard_map/all_gather | solution.py:71
  42.4 7.4 %copy-start.9 = (f32[3,256]{1,0:T(4,128)S(1)}, f32[3,256]{1,0:T(4,128)}, u32[]{:S(2)}) copy-start(f32[3,256]{1,0:T(4,128)} %param.25) | copy-start | bytes 9220
  42.4 7.5 %copy-start.6 = (s32[256]{0:T(256)S(1)}, s32[256]{0:T(256)}, u32[]{:S(2)}) copy-start(s32[256]{0:T(256)} %param.33) | copy-start | bytes 3076
  42.4 10.7 %copy-start.7 = (s32[4]{0:T(128)S(1)}, s32[4]{0:T(128)}, u32[]{:S(2)}) copy-start(s32[4]{0:T(128)} %param.34) | copy-start | bytes 52
  42.4 11.5 %copy-start.11 = (pred[4096]{0:T(1024)(128)(4,1)S(1)}, pred[4096]{0:T(1024)(128)(4,1)}, u32[]{:S(2)}) copy-start(pred[4096]{0:T(1024)(128)(4,1)} %constant.224) | copy-start | bytes 12292
  42.4 11.5 %copy-start.12 = (pred[4096]{0:T(1024)(128)(4,1)S(1)}, pred[4096]{0:T(1024)(128)(4,1)}, u32[]{:S(2)}) copy-start(pred[4096]{0:T(1024)(128)(4,1)} %constant.225) | copy-start | bytes 12292
  42.4 11.5 %copy-start.13 = (pred[4096]{0:T(1024)(128)(4,1)S(1)}, pred[4096]{0:T(1024)(128)(4,1)}, u32[]{:S(2)}) copy-start(pred[4096]{0:T(1024)(128)(4,1)} %constant.226) | copy-start | bytes 12292
  42.4 127.0 %all-to-all-start.1 = ((bf16[64,2,2,32,256]{4,3,2,1,0:T(8,128)(2,1)}), bf16[64,2,2,32,256]{4,3,2,1,0:T(8,128)(2,1)}, u32[]{:S(2)}, u32[]{:S(2)}) async-start(bf16[64,2,2,32,256]{4,3,2,1,0:T(8,128)(2,1)} %bitcast.72), calls=%async_computation.1 | async-start | bytes 8388608 | tf_op jit(solution)/shard_map/all_to_all | solution.py:94
  48.3 207.6 %all-gather.11.cloned.1.call-start = ((), (), s32[]{:S(2)}) async-start(), calls=%async_computation.4 | async-start | bytes 1064960 | tf_op jit(solution)/shard_map/all_gather | solution.py:128
  49.0 279.0 %all-gather.13.cloned.1.call-start = ((), (), s32[]{:S(2)}) async-start(), calls=%async_computation.5 | async-start | bytes 3194880 | tf_op jit(solution)/shard_map/all_gather | solution.py:141
  49.6 373.3 %all-gather.15.cloned.1.call-start = ((), (), s32[]{:S(2)}) async-start(), calls=%async_computation.6 | async-start | bytes 9437184 | tf_op jit(solution)/shard_map/all_gather | solution.py:132
  60.7 102.9 %copy-start.2 = (bf16[256,2048]{1,0:T(8,128)(2,1)S(1)}, bf16[256,2048]{1,0:T(8,128)(2,1)}, u32[]{:S(2)}) copy-start(bf16[256,2048]{1,0:T(8,128)(2,1)} %all-gather.7.cloned.1.call-done) | copy-start | bytes 3145732
  60.7 102.9 %copy-start.14 = (f32[2048]{0:T(1024)S(1)}, f32[2048]{0:T(1024)}, u32[]{:S(2)}) copy-start(f32[2048]{0:T(1024)} %param.23) | copy-start | bytes 24580
  60.7 102.8 %copy-start.15 = (f32[2048]{0:T(1024)S(1)}, f32[2048]{0:T(1024)}, u32[]{:S(2)}) copy-start(f32[2048]{0:T(1024)} %param.22) | copy-start | bytes 24580
  231.2 2.7 copy-start.5
  255.8 2.8 copy-start.10
  422.8 5.2 %copy-start.8 = (f32[2048]{0:T(1024)S(1)}, f32[2048]{0:T(1024)}, u32[]{:S(2)}) copy-start(f32[2048]{0:T(1024)} %param.28) | copy-start | bytes 24580
  428.1 3.1 copy-start.4
  428.1 3.1 copy-start.16
  428.1 3.0 copy-start.17
  430.2 1.0 copy-start.3
  430.6 4.4 copy-start.1
Sparse Core Ops, SparseCore 0:
  10.0 43.6 all-gather.6
  57.1 101.6 all-gather.8
  162.2 80.7 all-gather.10
  246.2 81.8 all-gather.12
  329.9 92.8 all-gather.14
